TPU v7x, 256 devices: a whole 4x4x8 slice. The times are simulated.
256 devices in a mesh: rows: 64 (over z, y, x_hi), cent: 4 (over x_lo, core).
Axes of the slice: x: 4 (x_hi: 2, x_lo: 2; x = x_hi * 2 + x_lo), y: 4, z: 8, core: 2. Of those that a mesh axis runs over, the one named last changes fastest.
Arguments:
- embeddings: bfloat16 [131072, 4096], P('rows', 'cent'), may hold values from -6 to 6
- basis: bfloat16 [4096, 512], P('cent'), may hold values from -0.09375 to 0.09375
- start_centroids: float32 [4096, 512], P('cent'), as said below
Outputs:
- centroids: float32 [4096, 512], P('cent')
- log_total: float32 [131072], P('rows')
Inputs may be any that keep to these rules, and one draw needn't show every extreme that they name: `start_centroids`: initial centroids, real-valued; some may lie far from the others.
All inputs are finite; a program needn't handle non-finite values.
Results may differ from a plain program's by a relative error of at most 0.0024.
The roundings to bfloat16 on the way count: a program that leaves them out, or rounds other values in their place, can miss the bound.
Values may be sent and summed in bfloat16 or wider, within the bound.
No kernel may reach another device: no remote copies, remote signals or barrier semaphores. Data moves between devices by JAX's collectives and lax.ppermute only.
A program may use at most 64 MiB of HBM per device.

v0:
```python
import jax
import jax.numpy as jnp
from jax import lax
from jax.sharding import Mesh
from jax.sharding import PartitionSpec as P

ITERS = 2
TEMPER = 8.0
ROW_AXES = ("z", "y", "xh")
CENT_AXES = ("xl", "core")


def _swap(x, axis, bit):
    size = {"y": 4, "xh": 2}[axis]
    return lax.ppermute(x, axis, [(i, i ^ bit) for i in range(size)])


def _bits():
    y = lax.axis_index("y")
    return ((y & 1, "y", 1), (y >> 1 & 1, "y", 2), (lax.axis_index("xh"), "xh", 1))


def _reduce_rows(numer, mass):
    count, width = numer.shape
    blocks = 8
    per = count // blocks
    mass_rows = (
        jnp.zeros((blocks, 8, width), jnp.float32).at[:, 0, :per].set(mass.reshape(blocks, per))
    )
    payload = jnp.concatenate([numer.reshape(blocks, per, width), mass_rows], axis=1)
    payload = payload.reshape(blocks * (per + 8), width)
    payload = lax.psum_scatter(payload, "z", scatter_dimension=0, tiled=True)
    numer, mass = (payload[:per], payload[per, :per])
    for bit, axis, mask in _bits():
        half = numer.shape[0] // 2
        keep = lax.dynamic_slice_in_dim(numer, bit * half, half, axis=0)
        send = lax.dynamic_slice_in_dim(numer, (1 - bit) * half, half, axis=0)
        keep_mass = lax.dynamic_slice_in_dim(mass, bit * half, half, axis=0)
        send_mass = lax.dynamic_slice_in_dim(mass, (1 - bit) * half, half, axis=0)
        numer = keep + _swap(send, axis, mask)
        mass = keep_mass + _swap(send_mass, axis, mask)
    return (numer, mass)


def _gather_rows(block):
    for bit, axis, mask in reversed(_bits()):
        other = _swap(block, axis, mask)
        block = jnp.where(
            bit == 0, jnp.concatenate([block, other]), jnp.concatenate([other, block])
        )
    return lax.all_gather(block, "z", axis=0, tiled=True)


def _row_offset(count):
    y = lax.axis_index("y")
    per = count // 64
    return (
        lax.axis_index("z") * (count // 8)
        + (y & 1) * (4 * per)
        + (y >> 1 & 1) * (2 * per)
        + lax.axis_index("xh") * per
    )


def _project(embeddings, basis):
    partial = jnp.dot(embeddings, basis, preferred_element_type=jnp.float32)
    steps = ((lax.axis_index("core"), "core"), (lax.axis_index("xl"), "xl"))
    for bit, axis in steps:
        half = partial.shape[0] // 2
        keep = lax.dynamic_slice_in_dim(partial, bit * half, half, axis=0)
        send = lax.dynamic_slice_in_dim(partial, (1 - bit) * half, half, axis=0)
        partial = keep + lax.ppermute(send, axis, [(0, 1), (1, 0)])
    block = partial.astype(jnp.bfloat16)
    for bit, axis in reversed(steps):
        other = lax.ppermute(block, axis, [(0, 1), (1, 0)])
        block = jnp.where(
            bit == 0, jnp.concatenate([block, other]), jnp.concatenate([other, block])
        )
    return block


def _merge(a, b):
    top = jnp.maximum(a[0], b[0])
    return jnp.stack([top, a[1] * jnp.exp(a[0] - top) + b[1] * jnp.exp(b[0] - top)])


def _log_total(scores):
    local_top = jnp.max(scores, axis=1)
    pair = jnp.stack([local_top, jnp.sum(jnp.exp(scores - local_top[:, None]), axis=1)])
    for axis in ("core", "xl"):
        other = lax.ppermute(pair, axis, [(0, 1), (1, 0)])
        low = lax.axis_index(axis) == 0
        pair = _merge(jnp.where(low, pair, other), jnp.where(low, other, pair))
    return pair[0] + jnp.log(pair[1])


def on_device(embeddings, basis, start_centroids):
    row_count = embeddings.shape[0]
    count = start_centroids.shape[0]
    per = count // 64
    projected = _project(embeddings, basis)
    start = _row_offset(count)
    block = lax.dynamic_slice_in_dim(start_centroids, start, per, axis=0)
    cent_bf = start_centroids.astype(jnp.bfloat16)
    log_total = jnp.zeros((row_count,), jnp.float32)
    for step in range(ITERS):
        scores = (
            lax.dot_general(
                projected, cent_bf, (((1,), (1,)), ((), ())), preferred_element_type=jnp.float32
            )
            / TEMPER
        )
        log_total = _log_total(scores)
        weights = jnp.exp(scores - log_total[:, None])
        local_mass = jnp.sum(weights, axis=0)
        local_numer = lax.dot_general(
            weights.astype(jnp.bfloat16),
            projected,
            (((0,), (0,)), ((), ())),
            preferred_element_type=jnp.float32,
        )
        numer, mass = _reduce_rows(local_numer, local_mass)
        block = (numer + block) / (mass[:, None] + 1.0)
        if step + 1 < ITERS:
            cent_bf = _gather_rows(block.astype(jnp.bfloat16))
    centroids = _gather_rows(block)
    return (centroids, log_total)


def solution(mesh):
    fine = Mesh(mesh.devices.reshape(8, 4, 2, 2, 2), ROW_AXES + CENT_AXES)
    return jax.shard_map(
        on_device,
        mesh=fine,
        in_specs=(P(ROW_AXES, CENT_AXES), P(CENT_AXES, None), P(CENT_AXES, None)),
        out_specs=(P(CENT_AXES, None), P(ROW_AXES)),
        check_vma=False,
    )
```

profile of v0, /device:TPU:2, one launch (start us, length us, event | category | flops | bytes accessed | tf_op | source)
XLA Modules:
  0.0 348.0 jit_solution(13008515234022563669)
XLA Ops:
  8.4 4.5 %fusion.34 = f32[2048,512]{1,0:T(8,128)S(1)} fusion(bf16[2048,1024]{1,0:T(8,128)(2,1)} %param.7, bf16[1024,512]{1,0:T(8,128)(2,1)S(1)} %copy-done), kind=kOutput, calls=%fused_computation.95 | convolution fusion | flops 2147483648 | bytes 9437184 | tf_op jit(solution)/shard_map/dot_general | solution.py:66
  15.2 4.3 %collective-permute-done = f32[1024,512]{1,0:T(8,128)} collective-permute-done((f32[1024,512]{1,0:T(8,128)S(1)}, f32[1024,512]{1,0:T(8,128)}, u32[]{:S(2)}, u32[]{:S(2)}) %collective-permute-start) | collective-permute-done | bytes 2097184 | tf_op jit(solution)/shard_map/ppermute | solution.py:72
  19.4 2.7 dynamic-slice_add_fusion
  25.4 23.8 %collective-permute-done.1 = f32[512,512]{1,0:T(8,128)} collective-permute-done((f32[512,512]{1,0:T(8,128)}, f32[512,512]{1,0:T(8,128)}, u32[]{:S(2)}, u32[]{:S(2)}) %collective-permute-start.1) | collective-permute-done | bytes 1048608 | tf_op jit(solution)/shard_map/ppermute | solution.py:72
  53.1 11.9 %collective-permute-done.2 = bf16[512,512]{1,0:T(8,128)(2,1)S(1)} collective-permute-done((bf16[512,512]{1,0:T(8,128)(2,1)}, bf16[512,512]{1,0:T(8,128)(2,1)S(1)}, u32[]{:S(2)}, u32[]{:S(2)}) %collective-permute-start.2) | collective-permute-done | bytes 524320 | tf_op jit(solution)/shard_map/ppermute | solution.py:75
  69.3 4.0 %multiply_reduce_fusion.1 = (f32[2048]{0:T(1024)S(1)}, f32[2048,1024]{0,1:T(8,128)S(1)}) fusion(f32[1024,512]{1,0:T(8,128)} %param.9, bf16[1024,512]{1,0:T(8,128)(2,1)S(1)} %collective-permute-done.3, bf16[1024,512]{1,0:T(8,128)(2,1)S(1)} %maximum_select_fusion.1, pred[]{:T(512)S(6)} %eq.25), kind=kOutput, calls=%fused_computation.9 | convolution fusion | flops 2161637376 | bytes 12591105 | tf_op jit(solution)/shard_map/dot_general | solution.py:108
  85.7 45.1 %reduce-scatter.3.cloned.1.call-done = f32[136,512]{1,0:T(8,128)} async-done(((f32[1088,512]{1,0:T(8,128)}), f32[136,512]{1,0:T(8,128)}) %reduce-scatter.3.cloned.1.call-update) | async-done | bytes 278544 | tf_op jit(solution)/shard_map/reduce_scatter | solution.py:32
  135.3 3.3 collective-permute-start.10
  139.2 2.9 collective-permute-start.7
  147.4 3.1 collective-permute-done.8
  153.6 3.1 collective-permute-done.12
  156.7 2.9 collective-permute-start.13
  163.5 3.0 collective-permute-done.14
  167.5 37.0 %all-gather.3.cloned.1.call-done = bf16[1024,512]{1,0:T(8,128)(2,1)} async-done(((bf16[128,512]{1,0:T(8,128)(2,1)}), bf16[1024,512]{1,0:T(8,128)(2,1)}) %all-gather.3.cloned.1.call-update) | async-done | bytes 1048592 | tf_op jit(solution)/shard_map/all_gather | solution.py:51
  204.6 3.6 %multiply_reduce_fusion = (f32[2048]{0:T(1024)S(1)}, f32[2048,1024]{0,1:T(8,128)S(1)}) fusion(bf16[1024,512]{1,0:T(8,128)(2,1)} %all-gather.3.cloned.1.call-done, bf16[1024,512]{1,0:T(8,128)(2,1)S(1)} %collective-permute-done.3, bf16[1024,512]{1,0:T(8,128)(2,1)S(1)} %maximum_select_fusion.1, pred[]{:T(512)S(6)} %eq.25), kind=kOutput, calls=%fused_computation.8 | convolution fusion | flops 2161113088 | bytes 11542529 | tf_op jit(solution)/shard_map/dot_general | solution.py:108
  211.6 3.2 collective-permute-done.16
  220.5 41.6 %reduce-scatter.5.cloned.1.call-done = f32[136,512]{1,0:T(8,128)} async-done(((f32[1088,512]{1,0:T(8,128)}), f32[136,512]{1,0:T(8,128)}) %reduce-scatter.5.cloned.1.call-update) | async-done | bytes 278544 | tf_op jit(solution)/shard_map/reduce_scatter | solution.py:32
  266.6 2.7 collective-permute-start.21
  278.6 3.4 collective-permute-done.19
  283.7 3.9 %collective-permute-done.23 = f32[16,512]{1,0:T(8,128)S(1)} collective-permute-done((f32[16,512]{1,0:T(8,128)S(1)}, f32[16,512]{1,0:T(8,128)S(1)}, u32[]{:S(2)}, u32[]{:S(2)}) %collective-permute-start.23) | collective-permute-done | bytes 32800 | tf_op jit(solution)/shard_map/ppermute | solution.py:15
  290.2 3.2 collective-permute-done.24
  294.2 4.3 %collective-permute-done.25 = f32[64,512]{1,0:T(8,128)S(1)} collective-permute-done((f32[64,512]{1,0:T(8,128)S(1)}, f32[64,512]{1,0:T(8,128)S(1)}, u32[]{:S(2)}, u32[]{:S(2)}) %collective-permute-start.25) | collective-permute-done | bytes 131104 | tf_op jit(solution)/shard_map/ppermute | solution.py:15
  299.2 39.2 %all-gather.5.cloned.1.call-done = f32[1024,512]{1,0:T(8,128)} async-done(((f32[128,512]{1,0:T(8,128)}), f32[1024,512]{1,0:T(8,128)}) %all-gather.5.cloned.1.call-update) | async-done | bytes 2097168 | tf_op jit(solution)/shard_map/all_gather | solution.py:51
  338.4 3.1 copy.6
  (112 shorter events, 74.2 us)
Async XLA Ops:
  7.2 123.7 %reduce-scatter.3.cloned.1.call-start = ((), (), s32[]{:S(2)}) async-start(), calls=%async_computation.2 | async-start | bytes 2506752 | tf_op jit(solution)/shard_map/reduce_scatter | solution.py:32
  15.1 4.4 %collective-permute-start = (f32[1024,512]{1,0:T(8,128)S(1)}, f32[1024,512]{1,0:T(8,128)}, u32[]{:S(2)}, u32[]{:S(2)}) collective-permute-start(f32[1024,512]{1,0:T(8,128)S(1)} %constant_dynamic-slice_fusion.11), channel_id=1, source_target_pairs={{0,1},{1,0},{2,3},{3,2},{4,5},{5,4},{6,7},{7,6},{8,9},{9,8},{10,11... | collective-permute-start | bytes 6291464 | tf_op jit(solution)/shard_map/ppermute | solution.py:72
  23.2 26.0 %collective-permute-start.1 = (f32[512,512]{1,0:T(8,128)}, f32[512,512]{1,0:T(8,128)}, u32[]{:S(2)}, u32[]{:S(2)}) collective-permute-start(f32[512,512]{1,0:T(8,128)} %constant_dynamic-slice_fusion.10), channel_id=1, source_target_pairs={{0,2},{2,0},{1,3},{3,1},{4,6},{6,4},{5,7},{7,5},{8,10},{10,8},{9,1... | collective-permute-start | bytes 3145736 | tf_op jit(solution)/shard_map/ppermute | solution.py:72
  51.4 13.6 %collective-permute-start.2 = (bf16[512,512]{1,0:T(8,128)(2,1)}, bf16[512,512]{1,0:T(8,128)(2,1)S(1)}, u32[]{:S(2)}, u32[]{:S(2)}) collective-permute-start(bf16[512,512]{1,0:T(8,128)(2,1)} %add_convert_fusion), channel_id=1, source_target_pairs={{0,2},{2,0},{1,3},{3,1},{4,6},{6,4},{5,7},{7,5},{8,10},{10,8},{9,1... | collective-permute-start | bytes 1572872 | tf_op jit(solution)/shard_map/ppermute | solution.py:75
  76.1 4.0 %collective-permute-start.5 = (f32[2,2048]{1,0:T(2,128)S(1)}, f32[2,2048]{1,0:T(2,128)S(1)}, u32[]{:S(2)}, u32[]{:S(2)}) collective-permute-start(f32[2,2048]{1,0:T(2,128)S(1)} %pad_maximum_fusion.1), channel_id=1, source_target_pairs={{0,2},{2,0},{1,3},{3,1},{4,6},{6,4},{5,7},{7,5},{8,10},{10,8},{9,1... | collective-permute-start | bytes 49160 | tf_op jit(solution)/shard_map/ppermute | solution.py:91
  85.6 118.9 %all-gather.3.cloned.1.call-start = ((), (), s32[]{:S(2)}) async-start(), calls=%async_computation.3 | async-start | bytes 1179648 | tf_op jit(solution)/shard_map/all_gather | solution.py:51
  134.1 5.1 %collective-permute-start.6 = (f32[64,512]{1,0:T(8,128)S(1)}, f32[64,512]{1,0:T(8,128)S(1)}, u32[]{:S(2)}, u32[]{:S(2)}) collective-permute-start(f32[64,512]{1,0:T(8,128)S(1)} %constant_dynamic-slice_fusion.9), channel_id=1, source_target_pairs={{0,8},{8,0},{16,24},{24,16},{1,9},{9,1},{17,25},{25,17},{2,10},{10... | collective-permute-start | bytes 393224 | tf_op jit(solution)/shard_map/ppermute | solution.py:15
  135.3 6.8 %collective-permute-start.10 = (f32[32]{0:T(128)S(1)}, f32[32]{0:T(128)S(1)}, u32[]{:S(2)}, u32[]{:S(2)}) collective-permute-start(f32[32]{0:T(128)S(1)} %dynamic_slice.111), channel_id=1, source_target_pairs={{0,16},{8,24},{16,0},{24,8},{1,17},{9,25},{17,1},{25,9},{2,18},{10... | collective-permute-start | bytes 392 | tf_op jit(solution)/shard_map/ppermute | solution.py:15
  139.2 5.9 %collective-permute-start.7 = (f32[32,512]{1,0:T(8,128)S(1)}, f32[32,512]{1,0:T(8,128)S(1)}, u32[]{:S(2)}, u32[]{:S(2)}) collective-permute-start(f32[32,512]{1,0:T(8,128)S(1)} %constant_dynamic-slice_fusion.8), channel_id=1, source_target_pairs={{0,16},{8,24},{16,0},{24,8},{1,17},{9,25},{17,1},{25,9},{2,18},{10... | collective-permute-start | bytes 196616 | tf_op jit(solution)/shard_map/ppermute | solution.py:15
  142.2 5.1 %collective-permute-start.11 = (f32[16]{0:T(128)S(1)}, f32[16]{0:T(128)S(1)}, u32[]{:S(2)}, u32[]{:S(2)}) collective-permute-start(f32[16]{0:T(128)S(1)} %dynamic_slice.113), channel_id=1, source_target_pairs={{0,4},{4,0},{1,5},{5,1},{2,6},{6,2},{3,7},{7,3},{8,12},{12,8},{9,1... | collective-permute-start | bytes 200 | tf_op jit(solution)/shard_map/ppermute | solution.py:15
  145.0 5.5 %collective-permute-start.8 = (f32[16,512]{1,0:T(8,128)S(1)}, f32[16,512]{1,0:T(8,128)S(1)}, u32[]{:S(2)}, u32[]{:S(2)}) collective-permute-start(f32[16,512]{1,0:T(8,128)S(1)} %constant_dynamic-slice_fusion.6), channel_id=1, source_target_pairs={{0,4},{4,0},{1,5},{5,1},{2,6},{6,2},{3,7},{7,3},{8,12},{12,8},{9,1... | collective-permute-start | bytes 98312 | tf_op jit(solution)/shard_map/ppermute | solution.py:15
  151.4 5.3 %collective-permute-start.12 = (bf16[16,512]{1,0:T(8,128)(2,1)S(1)}, bf16[16,512]{1,0:T(8,128)(2,1)S(1)}, u32[]{:S(2)}, u32[]{:S(2)}) collective-permute-start(bf16[16,512]{1,0:T(8,128)(2,1)S(1)} %get-tuple-element.28), channel_id=1, source_target_pairs={{0,4},{4,0},{1,5},{5,1},{2,6},{6,2},{3,7},{7,3},{8,12},{12,8},{9,1... | collective-permute-start | bytes 49160 | tf_op jit(solution)/shard_map/ppermute | solution.py:15
  156.7 5.5 %collective-permute-start.13 = (bf16[32,512]{1,0:T(8,128)(2,1)S(1)}, bf16[32,512]{1,0:T(8,128)(2,1)S(1)}, u32[]{:S(2)}, u32[]{:S(2)}) collective-permute-start(bf16[32,512]{1,0:T(8,128)(2,1)S(1)} %maximum_select_fusion.7), channel_id=1, source_target_pairs={{0,16},{8,24},{16,0},{24,8},{1,17},{9,25},{17,1},{25,9},{2,18},{10... | collective-permute-start | bytes 98312 | tf_op jit(solution)/shard_map/ppermute | solution.py:15
  162.2 4.4 %collective-permute-start.14 = (bf16[64,512]{1,0:T(8,128)(2,1)S(1)}, bf16[64,512]{1,0:T(8,128)(2,1)S(1)}, u32[]{:S(2)}, u32[]{:S(2)}) collective-permute-start(bf16[64,512]{1,0:T(8,128)(2,1)S(1)} %maximum_select_fusion.5), channel_id=1, source_target_pairs={{0,8},{8,0},{16,24},{24,16},{1,9},{9,1},{17,25},{25,17},{2,10},{10... | collective-permute-start | bytes 196616 | tf_op jit(solution)/shard_map/ppermute | solution.py:15
  167.3 94.8 %reduce-scatter.5.cloned.1.call-start = ((), (), s32[]{:S(2)}) async-start(), calls=%async_computation.4 | async-start | bytes 2506752 | tf_op jit(solution)/shard_map/reduce_scatter | solution.py:32
  220.4 118.0 %all-gather.5.cloned.1.call-start = ((), (), s32[]{:S(2)}) async-start(), calls=%async_computation.5 | async-start | bytes 2359296 | tf_op jit(solution)/shard_map/all_gather | solution.py:51
  265.5 5.1 %collective-permute-start.17 = (f32[64,512]{1,0:T(8,128)S(1)}, f32[64,512]{1,0:T(8,128)S(1)}, u32[]{:S(2)}, u32[]{:S(2)}) collective-permute-start(f32[64,512]{1,0:T(8,128)S(1)} %constant_dynamic-slice_fusion.3), channel_id=1, source_target_pairs={{0,8},{8,0},{16,24},{24,16},{1,9},{9,1},{17,25},{25,17},{2,10},{10... | collective-permute-start | bytes 393224 | tf_op jit(solution)/shard_map/ppermute | solution.py:15
  266.6 6.8 %collective-permute-start.21 = (f32[32]{0:T(128)S(1)}, f32[32]{0:T(128)S(1)}, u32[]{:S(2)}, u32[]{:S(2)}) collective-permute-start(f32[32]{0:T(128)S(1)} %dynamic_slice.125), channel_id=1, source_target_pairs={{0,16},{8,24},{16,0},{24,8},{1,17},{9,25},{17,1},{25,9},{2,18},{10... | collective-permute-start | bytes 392 | tf_op jit(solution)/shard_map/ppermute | solution.py:15
  270.6 5.9 %collective-permute-start.18 = (f32[32,512]{1,0:T(8,128)S(1)}, f32[32,512]{1,0:T(8,128)S(1)}, u32[]{:S(2)}, u32[]{:S(2)}) collective-permute-start(f32[32,512]{1,0:T(8,128)S(1)} %constant_dynamic-slice_fusion.2), channel_id=1, source_target_pairs={{0,16},{8,24},{16,0},{24,8},{1,17},{9,25},{17,1},{25,9},{2,18},{10... | collective-permute-start | bytes 196616 | tf_op jit(solution)/shard_map/ppermute | solution.py:15
  273.5 5.1 %collective-permute-start.22 = (f32[16]{0:T(128)S(1)}, f32[16]{0:T(128)S(1)}, u32[]{:S(2)}, u32[]{:S(2)}) collective-permute-start(f32[16]{0:T(128)S(1)} %dynamic_slice.127), channel_id=1, source_target_pairs={{0,4},{4,0},{1,5},{5,1},{2,6},{6,2},{3,7},{7,3},{8,12},{12,8},{9,1... | collective-permute-start | bytes 200 | tf_op jit(solution)/shard_map/ppermute | solution.py:15
  276.5 5.5 %collective-permute-start.19 = (f32[16,512]{1,0:T(8,128)S(1)}, f32[16,512]{1,0:T(8,128)S(1)}, u32[]{:S(2)}, u32[]{:S(2)}) collective-permute-start(f32[16,512]{1,0:T(8,128)S(1)} %constant_dynamic-slice_fusion.1), channel_id=1, source_target_pairs={{0,4},{4,0},{1,5},{5,1},{2,6},{6,2},{3,7},{7,3},{8,12},{12,8},{9,1... | collective-permute-start | bytes 98312 | tf_op jit(solution)/shard_map/ppermute | solution.py:15
  282.1 5.4 %collective-permute-start.23 = (f32[16,512]{1,0:T(8,128)S(1)}, f32[16,512]{1,0:T(8,128)S(1)}, u32[]{:S(2)}, u32[]{:S(2)}) collective-permute-start(f32[16,512]{1,0:T(8,128)S(1)} %add_divide_fusion), channel_id=1, source_target_pairs={{0,4},{4,0},{1,5},{5,1},{2,6},{6,2},{3,7},{7,3},{8,12},{12,8},{9,1... | collective-permute-start | bytes 98312 | tf_op jit(solution)/shard_map/ppermute | solution.py:15
  287.6 5.9 %collective-permute-start.24 = (f32[32,512]{1,0:T(8,128)S(1)}, f32[32,512]{1,0:T(8,128)S(1)}, u32[]{:S(2)}, u32[]{:S(2)}) collective-permute-start(f32[32,512]{1,0:T(8,128)S(1)} %maximum_select_fusion.6), channel_id=1, source_target_pairs={{0,16},{8,24},{16,0},{24,8},{1,17},{9,25},{17,1},{25,9},{2,18},{10... | collective-permute-start | bytes 196616 | tf_op jit(solution)/shard_map/ppermute | solution.py:15
  293.4 5.1 %collective-permute-start.25 = (f32[64,512]{1,0:T(8,128)S(1)}, f32[64,512]{1,0:T(8,128)S(1)}, u32[]{:S(2)}, u32[]{:S(2)}) collective-permute-start(f32[64,512]{1,0:T(8,128)S(1)} %maximum_select_fusion.4), channel_id=1, source_target_pairs={{0,8},{8,0},{16,24},{24,16},{1,9},{9,1},{17,25},{25,17},{2,10},{10... | collective-permute-start | bytes 393224 | tf_op jit(solution)/shard_map/ppermute | solution.py:15
  (9 other events, 20.9 us)
Sparse Core Ops, SparseCore 0:
  85.7 45.0 reduce-scatter.2
  167.4 37.1 all-gather.2
  220.5 41.5 reduce-scatter.4
  299.4 39.0 all-gather.4
where the time goes:
time: 349 us; the launch traced here: 348 us
  waiting for transfers between devices  245 us (70%)
  starting transfers between devices  42.1 us (12%)
  other arithmetic  18.4 us (5%)
  matrix products  16.9 us (5%)
  between operations  14.1 us (4%)
  local copies, waits for them, and re-layouts  11.3 us (3%)
    reduce_scatter x2, waiting for transfers between devices, _reduce_rows(): payload = lax.psum_scatter(payload, 'z', scatter_dimension=0, tiled=True)  86.8 us
    all_gather x2, waiting for transfers between devices, _gather_rows(): return lax.all_gather(block, 'z', axis=0, tiled=True)  76.2 us
    ppermute x18, starting transfers between devices, _swap(): return lax.ppermute(x, axis, [(i, i ^ bit) for i in range(size)])  34.9 us
    ppermute x18, waiting for transfers between devices, _swap(): return lax.ppermute(x, axis, [(i, i ^ bit) for i in range(size)])  31.9 us
    ppermute x2, waiting for transfers between devices, _project(): partial = keep + lax.ppermute(send, axis, [(0, 1), (1, 0)])  28 us
    ppermute x2, waiting for transfers between devices, _project(): other = lax.ppermute(block, axis, [(0, 1), (1, 0)])  14.5 us
    ppermute x4, waiting for transfers between devices, _log_total(): other = lax.ppermute(pair, axis, [(0, 1), (1, 0)])  7.67 us
    dot_general x2, matrix products, on_device(): lax.dot_general(projected, cent_bf, (((1,), (1,)), ((), ())), preferred_e...  7.58 us
  transfers between devices with their start and end apart: 30, of which 27 were waited for; matrix products, arithmetic and copies ran while one was open for 1% of the time, Pallas kernels for 0%

commit v1 on v0

--- a/solution.py
+++ b/solution.py
@@ -48,7 +48,19 @@
         block = jnp.where(
             bit == 0, jnp.concatenate([block, other]), jnp.concatenate([other, block])
         )
-    return lax.all_gather(block, "z", axis=0, tiled=True)
+
+    def flows_unite(in_array, group_axis):
+        return jnp.concatenate(
+            jax.lax.all_to_all(
+                jnp.stack([in_array] * jax.lax.axis_size(group_axis), axis=0),
+                group_axis,
+                split_axis=0,
+                concat_axis=0,
+            ),
+            axis=0,
+        )
+
+    return flows_unite(block, "z")
 
 
 def _row_offset(count):

time: 349 us -> 334 us (0.957)
  waiting for transfers between devices: 245 us -> 164 us
  blocking collectives: 0 us -> 69.1 us
    all_gather x2 -> x0, waiting for transfers between devices: 76.2 us -> none  [_gather_rows(): return lax.all_gather(block, 'z', axis=0, tiled=True)]
    all_to_all x0 -> x2, blocking collectives: none -> 69.1 us  [flows_unite(): jax.lax.all_to_all(jnp.stack([in_array] * jax.lax.axis_size(group_axis),...]
  transfers between devices with their start and end apart: 30 -> 28, of which waited for: 27 -> 24; matrix products, arithmetic and copies ran while one was open for 1% -> 1% of each run, Pallas kernels for 0% -> 0%
where the time goes in v1:
time: 334 us
  waiting for transfers between devices  164 us (49%)
  blocking collectives  69.1 us (21%)
  starting transfers between devices  43.4 us (13%)
  other arithmetic  17.1 us (5%)
  matrix products  15.7 us (5%)
  between operations  14.4 us (4%)
  local copies, waits for them, and re-layouts  9.86 us (3%)
    reduce_scatter x2, waiting for transfers between devices, _reduce_rows(): payload = lax.psum_scatter(payload, 'z', scatter_dimension=0, tiled=True)  83.5 us
    all_to_all x2, blocking collectives, flows_unite(): jax.lax.all_to_all(jnp.stack([in_array] * jax.lax.axis_size(group_axis),...  69.1 us
    ppermute x18, starting transfers between devices, _swap(): return lax.ppermute(x, axis, [(i, i ^ bit) for i in range(size)])  36.7 us
    ppermute x18, waiting for transfers between devices, _swap(): return lax.ppermute(x, axis, [(i, i ^ bit) for i in range(size)])  29.9 us
    ppermute x2, waiting for transfers between devices, _project(): partial = keep + lax.ppermute(send, axis, [(0, 1), (1, 0)])  28 us
    ppermute x2, waiting for transfers between devices, _project(): other = lax.ppermute(block, axis, [(0, 1), (1, 0)])  14.5 us
    ppermute x4, waiting for transfers between devices, _log_total(): other = lax.ppermute(pair, axis, [(0, 1), (1, 0)])  7.96 us
  transfers between devices with their start and end apart: 28, of which 24 were waited for; matrix products, arithmetic and copies ran while one was open for 1% of the time, Pallas kernels for 0%

profile of v1, /device:TPU:2, one launch (start us, length us, event | category | flops | bytes accessed | tf_op | source)
XLA Modules:
  0.0 333.5 jit_solution(8118744879258195521)
XLA Ops:
  8.4 4.5 %fusion.34 = f32[2048,512]{1,0:T(8,128)S(1)} fusion(bf16[2048,1024]{1,0:T(8,128)(2,1)} %param.7, bf16[1024,512]{1,0:T(8,128)(2,1)S(1)} %copy-done), kind=kOutput, calls=%fused_computation.95 | convolution fusion | flops 2147483648 | bytes 9437184 | tf_op jit(solution)/shard_map/dot_general | solution.py:78
  15.2 4.3 %collective-permute-done = f32[1024,512]{1,0:T(8,128)} collective-permute-done((f32[1024,512]{1,0:T(8,128)S(1)}, f32[1024,512]{1,0:T(8,128)}, u32[]{:S(2)}, u32[]{:S(2)}) %collective-permute-start) | collective-permute-done | bytes 2097184 | tf_op jit(solution)/shard_map/ppermute | solution.py:84
  19.4 2.7 dynamic-slice_add_fusion
  25.4 23.8 %collective-permute-done.1 = f32[512,512]{1,0:T(8,128)} collective-permute-done((f32[512,512]{1,0:T(8,128)}, f32[512,512]{1,0:T(8,128)}, u32[]{:S(2)}, u32[]{:S(2)}) %collective-permute-start.1) | collective-permute-done | bytes 1048608 | tf_op jit(solution)/shard_map/ppermute | solution.py:84
  53.1 11.9 %collective-permute-done.2 = bf16[512,512]{1,0:T(8,128)(2,1)S(1)} collective-permute-done((bf16[512,512]{1,0:T(8,128)(2,1)}, bf16[512,512]{1,0:T(8,128)(2,1)S(1)}, u32[]{:S(2)}, u32[]{:S(2)}) %collective-permute-start.2) | collective-permute-done | bytes 524320 | tf_op jit(solution)/shard_map/ppermute | solution.py:87
  69.3 4.0 %multiply_reduce_fusion.1 = (f32[2048]{0:T(1024)S(1)}, f32[2048,1024]{0,1:T(8,128)S(1)}) fusion(f32[1024,512]{1,0:T(8,128)} %param.9, bf16[1024,512]{1,0:T(8,128)(2,1)S(1)} %collective-permute-done.3, bf16[1024,512]{1,0:T(8,128)(2,1)S(1)} %maximum_select_fusion.1, pred[]{:T(512)S(6)} %eq.25), kind=kOutput, calls=%fused_computation.9 | convolution fusion | flops 2161637376 | bytes 12591105 | tf_op jit(solution)/shard_map/dot_general | solution.py:120
  85.7 45.1 %reduce-scatter.3.cloned.1.call-done = f32[136,512]{1,0:T(8,128)} async-done(((f32[1088,512]{1,0:T(8,128)}), f32[136,512]{1,0:T(8,128)}) %reduce-scatter.3.cloned.1.call-update) | async-done | bytes 278544 | tf_op jit(solution)/shard_map/reduce_scatter | solution.py:32
  135.3 3.3 collective-permute-start.10
  139.1 2.9 collective-permute-start.7
  147.4 3.1 collective-permute-done.8
  153.6 3.1 collective-permute-done.12
  156.7 2.9 collective-permute-start.13
  163.5 3.0 collective-permute-done.14
  166.6 24.1 %all_to_all.10 = bf16[8,128,512]{2,1,0:T(8,128)(2,1)S(1)} all-to-all(bf16[8,128,512]{2,1,0:T(8,128)(2,1)S(1)} %stack.24), channel_id=1, replica_groups=mesh['z'=8,'y'=4,'xh'=2,'xl'=2,'core'=2] {'z'}, dimensions={0} | all-to-all | bytes 2097152 | tf_op jit(solution)/shard_map/all_to_all | solution.py:54
  196.3 3.5 %collective-permute-done.16 = f32[2,2048]{1,0:T(2,128)S(1)} collective-permute-done((f32[2,2048]{1,0:T(2,128)S(1)}, f32[2,2048]{1,0:T(2,128)S(1)}, u32[]{:S(2)}, u32[]{:S(2)}) %collective-permute-start.16) | collective-permute-done | bytes 16416 | tf_op jit(solution)/shard_map/ppermute | solution.py:103
  205.3 38.4 %reduce-scatter.5.cloned.1.call-done = f32[136,512]{1,0:T(8,128)} async-done(((f32[1088,512]{1,0:T(8,128)}), f32[136,512]{1,0:T(8,128)}) %reduce-scatter.5.cloned.1.call-update) | async-done | bytes 278544 | tf_op jit(solution)/shard_map/reduce_scatter | solution.py:32
  248.2 3.0 collective-permute-start.21
  252.2 2.7 collective-permute-start.18
  260.2 3.4 %collective-permute-done.19 = f32[16,512]{1,0:T(8,128)S(1)} collective-permute-done((f32[16,512]{1,0:T(8,128)S(1)}, f32[16,512]{1,0:T(8,128)S(1)}, u32[]{:S(2)}, u32[]{:S(2)}) %collective-permute-start.19) | collective-permute-done | bytes 32800 | tf_op jit(solution)/shard_map/ppermute | solution.py:15
  265.6 3.5 %collective-permute-done.23 = f32[16,512]{1,0:T(8,128)S(1)} collective-permute-done((f32[16,512]{1,0:T(8,128)S(1)}, f32[16,512]{1,0:T(8,128)S(1)}, u32[]{:S(2)}, u32[]{:S(2)}) %collective-permute-start.23) | collective-permute-done | bytes 32800 | tf_op jit(solution)/shard_map/ppermute | solution.py:15
  269.1 2.7 collective-permute-start.24
  271.8 3.2 collective-permute-done.24
  276.2 3.9 %collective-permute-done.25 = f32[64,512]{1,0:T(8,128)S(1)} collective-permute-done((f32[64,512]{1,0:T(8,128)S(1)}, f32[64,512]{1,0:T(8,128)S(1)}, u32[]{:S(2)}, u32[]{:S(2)}) %collective-permute-start.25) | collective-permute-done | bytes 131104 | tf_op jit(solution)/shard_map/ppermute | solution.py:15
  280.3 45.0 %all_to_all.11 = f32[8,128,512]{2,1,0:T(8,128)S(1)} all-to-all(f32[8,128,512]{2,1,0:T(8,128)S(1)} %stack.29), channel_id=1, replica_groups=mesh['z'=8,'y'=4,'xh'=2,'xl'=2,'core'=2] {'z'}, dimensions={0} | all-to-all | bytes 4194304 | tf_op jit(solution)/shard_map/all_to_all | solution.py:54
  (110 shorter events, 71.3 us)
Async XLA Ops:
  7.2 123.6 %reduce-scatter.3.cloned.1.call-start = ((), (), s32[]{:S(2)}) async-start(), calls=%async_computation.4 | async-start | bytes 2506752 | tf_op jit(solution)/shard_map/reduce_scatter | solution.py:32
  15.0 4.4 %collective-permute-start = (f32[1024,512]{1,0:T(8,128)S(1)}, f32[1024,512]{1,0:T(8,128)}, u32[]{:S(2)}, u32[]{:S(2)}) collective-permute-start(f32[1024,512]{1,0:T(8,128)S(1)} %constant_dynamic-slice_fusion.11), channel_id=1, source_target_pairs={{0,1},{1,0},{2,3},{3,2},{4,5},{5,4},{6,7},{7,6},{8,9},{9,8},{10,11... | collective-permute-start | bytes 6291464 | tf_op jit(solution)/shard_map/ppermute | solution.py:84
  23.2 26.0 %collective-permute-start.1 = (f32[512,512]{1,0:T(8,128)}, f32[512,512]{1,0:T(8,128)}, u32[]{:S(2)}, u32[]{:S(2)}) collective-permute-start(f32[512,512]{1,0:T(8,128)} %constant_dynamic-slice_fusion.10), channel_id=1, source_target_pairs={{0,2},{2,0},{1,3},{3,1},{4,6},{6,4},{5,7},{7,5},{8,10},{10,8},{9,1... | collective-permute-start | bytes 3145736 | tf_op jit(solution)/shard_map/ppermute | solution.py:84
  51.4 13.6 %collective-permute-start.2 = (bf16[512,512]{1,0:T(8,128)(2,1)}, bf16[512,512]{1,0:T(8,128)(2,1)S(1)}, u32[]{:S(2)}, u32[]{:S(2)}) collective-permute-start(bf16[512,512]{1,0:T(8,128)(2,1)} %add_convert_fusion), channel_id=1, source_target_pairs={{0,2},{2,0},{1,3},{3,1},{4,6},{6,4},{5,7},{7,5},{8,10},{10,8},{9,1... | collective-permute-start | bytes 1572872 | tf_op jit(solution)/shard_map/ppermute | solution.py:87
  76.1 4.0 %collective-permute-start.5 = (f32[2,2048]{1,0:T(2,128)S(1)}, f32[2,2048]{1,0:T(2,128)S(1)}, u32[]{:S(2)}, u32[]{:S(2)}) collective-permute-start(f32[2,2048]{1,0:T(2,128)S(1)} %pad_maximum_fusion.1), channel_id=1, source_target_pairs={{0,2},{2,0},{1,3},{3,1},{4,6},{6,4},{5,7},{7,5},{8,10},{10,8},{9,1... | collective-permute-start | bytes 49160 | tf_op jit(solution)/shard_map/ppermute | solution.py:103
  85.6 158.1 %reduce-scatter.5.cloned.1.call-start = ((), (), s32[]{:S(2)}) async-start(), calls=%async_computation.5 | async-start | bytes 2506752 | tf_op jit(solution)/shard_map/reduce_scatter | solution.py:32
  131.6 3.6 %collective-permute-start.9 = (f32[64]{0:T(128)S(1)}, f32[64]{0:T(128)S(1)}, u32[]{:S(2)}, u32[]{:S(2)}) collective-permute-start(f32[64]{0:T(128)S(1)} %fusion.23), channel_id=1, source_target_pairs={{0,8},{8,0},{16,24},{24,16},{1,9},{9,1},{17,25},{25,17},{2,10},{10... | collective-permute-start | bytes 776 | tf_op jit(solution)/shard_map/ppermute | solution.py:15
  134.0 5.1 %collective-permute-start.6 = (f32[64,512]{1,0:T(8,128)S(1)}, f32[64,512]{1,0:T(8,128)S(1)}, u32[]{:S(2)}, u32[]{:S(2)}) collective-permute-start(f32[64,512]{1,0:T(8,128)S(1)} %constant_dynamic-slice_fusion.9), channel_id=1, source_target_pairs={{0,8},{8,0},{16,24},{24,16},{1,9},{9,1},{17,25},{25,17},{2,10},{10... | collective-permute-start | bytes 393224 | tf_op jit(solution)/shard_map/ppermute | solution.py:15
  135.3 6.8 %collective-permute-start.10 = (f32[32]{0:T(128)S(1)}, f32[32]{0:T(128)S(1)}, u32[]{:S(2)}, u32[]{:S(2)}) collective-permute-start(f32[32]{0:T(128)S(1)} %dynamic_slice.111), channel_id=1, source_target_pairs={{0,16},{8,24},{16,0},{24,8},{1,17},{9,25},{17,1},{25,9},{2,18},{10... | collective-permute-start | bytes 392 | tf_op jit(solution)/shard_map/ppermute | solution.py:15
  139.1 5.9 %collective-permute-start.7 = (f32[32,512]{1,0:T(8,128)S(1)}, f32[32,512]{1,0:T(8,128)S(1)}, u32[]{:S(2)}, u32[]{:S(2)}) collective-permute-start(f32[32,512]{1,0:T(8,128)S(1)} %constant_dynamic-slice_fusion.8), channel_id=1, source_target_pairs={{0,16},{8,24},{16,0},{24,8},{1,17},{9,25},{17,1},{25,9},{2,18},{10... | collective-permute-start | bytes 196616 | tf_op jit(solution)/shard_map/ppermute | solution.py:15
  142.2 5.1 %collective-permute-start.11 = (f32[16]{0:T(128)S(1)}, f32[16]{0:T(128)S(1)}, u32[]{:S(2)}, u32[]{:S(2)}) collective-permute-start(f32[16]{0:T(128)S(1)} %dynamic_slice.113), channel_id=1, source_target_pairs={{0,4},{4,0},{1,5},{5,1},{2,6},{6,2},{3,7},{7,3},{8,12},{12,8},{9,1... | collective-permute-start | bytes 200 | tf_op jit(solution)/shard_map/ppermute | solution.py:15
  145.0 5.5 %collective-permute-start.8 = (f32[16,512]{1,0:T(8,128)S(1)}, f32[16,512]{1,0:T(8,128)S(1)}, u32[]{:S(2)}, u32[]{:S(2)}) collective-permute-start(f32[16,512]{1,0:T(8,128)S(1)} %constant_dynamic-slice_fusion.6), channel_id=1, source_target_pairs={{0,4},{4,0},{1,5},{5,1},{2,6},{6,2},{3,7},{7,3},{8,12},{12,8},{9,1... | collective-permute-start | bytes 98312 | tf_op jit(solution)/shard_map/ppermute | solution.py:15
  151.4 5.3 %collective-permute-start.12 = (bf16[16,512]{1,0:T(8,128)(2,1)S(1)}, bf16[16,512]{1,0:T(8,128)(2,1)S(1)}, u32[]{:S(2)}, u32[]{:S(2)}) collective-permute-start(bf16[16,512]{1,0:T(8,128)(2,1)S(1)} %get-tuple-element.28), channel_id=1, source_target_pairs={{0,4},{4,0},{1,5},{5,1},{2,6},{6,2},{3,7},{7,3},{8,12},{12,8},{9,1... | collective-permute-start | bytes 49160 | tf_op jit(solution)/shard_map/ppermute | solution.py:15
  156.7 5.5 %collective-permute-start.13 = (bf16[32,512]{1,0:T(8,128)(2,1)S(1)}, bf16[32,512]{1,0:T(8,128)(2,1)S(1)}, u32[]{:S(2)}, u32[]{:S(2)}) collective-permute-start(bf16[32,512]{1,0:T(8,128)(2,1)S(1)} %maximum_select_fusion.7), channel_id=1, source_target_pairs={{0,16},{8,24},{16,0},{24,8},{1,17},{9,25},{17,1},{25,9},{2,18},{10... | collective-permute-start | bytes 98312 | tf_op jit(solution)/shard_map/ppermute | solution.py:15
  162.2 4.4 %collective-permute-start.14 = (bf16[64,512]{1,0:T(8,128)(2,1)S(1)}, bf16[64,512]{1,0:T(8,128)(2,1)S(1)}, u32[]{:S(2)}, u32[]{:S(2)}) collective-permute-start(bf16[64,512]{1,0:T(8,128)(2,1)S(1)} %maximum_select_fusion.5), channel_id=1, source_target_pairs={{0,8},{8,0},{16,24},{24,16},{1,9},{9,1},{17,25},{25,17},{2,10},{10... | collective-permute-start | bytes 196616 | tf_op jit(solution)/shard_map/ppermute | solution.py:15
  195.9 3.8 %collective-permute-start.16 = (f32[2,2048]{1,0:T(2,128)S(1)}, f32[2,2048]{1,0:T(2,128)S(1)}, u32[]{:S(2)}, u32[]{:S(2)}) collective-permute-start(f32[2,2048]{1,0:T(2,128)S(1)} %pad_maximum_fusion.3), channel_id=1, source_target_pairs={{0,2},{2,0},{1,3},{3,1},{4,6},{6,4},{5,7},{7,5},{8,10},{10,8},{9,1... | collective-permute-start | bytes 49160 | tf_op jit(solution)/shard_map/ppermute | solution.py:103
  246.9 5.2 %collective-permute-start.17 = (f32[64,512]{1,0:T(8,128)S(1)}, f32[64,512]{1,0:T(8,128)S(1)}, u32[]{:S(2)}, u32[]{:S(2)}) collective-permute-start(f32[64,512]{1,0:T(8,128)S(1)} %constant_dynamic-slice_fusion.3), channel_id=1, source_target_pairs={{0,8},{8,0},{16,24},{24,16},{1,9},{9,1},{17,25},{25,17},{2,10},{10... | collective-permute-start | bytes 393224 | tf_op jit(solution)/shard_map/ppermute | solution.py:15
  248.2 6.7 %collective-permute-start.21 = (f32[32]{0:T(128)S(1)}, f32[32]{0:T(128)S(1)}, u32[]{:S(2)}, u32[]{:S(2)}) collective-permute-start(f32[32]{0:T(128)S(1)} %dynamic_slice.125), channel_id=1, source_target_pairs={{0,16},{8,24},{16,0},{24,8},{1,17},{9,25},{17,1},{25,9},{2,18},{10... | collective-permute-start | bytes 392 | tf_op jit(solution)/shard_map/ppermute | solution.py:15
  252.2 5.9 %collective-permute-start.18 = (f32[32,512]{1,0:T(8,128)S(1)}, f32[32,512]{1,0:T(8,128)S(1)}, u32[]{:S(2)}, u32[]{:S(2)}) collective-permute-start(f32[32,512]{1,0:T(8,128)S(1)} %constant_dynamic-slice_fusion.2), channel_id=1, source_target_pairs={{0,16},{8,24},{16,0},{24,8},{1,17},{9,25},{17,1},{25,9},{2,18},{10... | collective-permute-start | bytes 196616 | tf_op jit(solution)/shard_map/ppermute | solution.py:15
  255.0 5.1 %collective-permute-start.22 = (f32[16]{0:T(128)S(1)}, f32[16]{0:T(128)S(1)}, u32[]{:S(2)}, u32[]{:S(2)}) collective-permute-start(f32[16]{0:T(128)S(1)} %dynamic_slice.127), channel_id=1, source_target_pairs={{0,4},{4,0},{1,5},{5,1},{2,6},{6,2},{3,7},{7,3},{8,12},{12,8},{9,1... | collective-permute-start | bytes 200 | tf_op jit(solution)/shard_map/ppermute | solution.py:15
  258.1 5.5 %collective-permute-start.19 = (f32[16,512]{1,0:T(8,128)S(1)}, f32[16,512]{1,0:T(8,128)S(1)}, u32[]{:S(2)}, u32[]{:S(2)}) collective-permute-start(f32[16,512]{1,0:T(8,128)S(1)} %constant_dynamic-slice_fusion.1), channel_id=1, source_target_pairs={{0,4},{4,0},{1,5},{5,1},{2,6},{6,2},{3,7},{7,3},{8,12},{12,8},{9,1... | collective-permute-start | bytes 98312 | tf_op jit(solution)/shard_map/ppermute | solution.py:15
  263.7 5.4 %collective-permute-start.23 = (f32[16,512]{1,0:T(8,128)S(1)}, f32[16,512]{1,0:T(8,128)S(1)}, u32[]{:S(2)}, u32[]{:S(2)}) collective-permute-start(f32[16,512]{1,0:T(8,128)S(1)} %add_divide_fusion), channel_id=1, source_target_pairs={{0,4},{4,0},{1,5},{5,1},{2,6},{6,2},{3,7},{7,3},{8,12},{12,8},{9,1... | collective-permute-start | bytes 98312 | tf_op jit(solution)/shard_map/ppermute | solution.py:15
  269.1 5.9 %collective-permute-start.24 = (f32[32,512]{1,0:T(8,128)S(1)}, f32[32,512]{1,0:T(8,128)S(1)}, u32[]{:S(2)}, u32[]{:S(2)}) collective-permute-start(f32[32,512]{1,0:T(8,128)S(1)} %maximum_select_fusion.6), channel_id=1, source_target_pairs={{0,16},{8,24},{16,0},{24,8},{1,17},{9,25},{17,1},{25,9},{2,18},{10... | collective-permute-start | bytes 196616 | tf_op jit(solution)/shard_map/ppermute | solution.py:15
  275.0 5.1 %collective-permute-start.25 = (f32[64,512]{1,0:T(8,128)S(1)}, f32[64,512]{1,0:T(8,128)S(1)}, u32[]{:S(2)}, u32[]{:S(2)}) collective-permute-start(f32[64,512]{1,0:T(8,128)S(1)} %maximum_select_fusion.4), channel_id=1, source_target_pairs={{0,8},{8,0},{16,24},{24,16},{1,9},{9,1},{17,25},{25,17},{2,10},{10... | collective-permute-start | bytes 393224 | tf_op jit(solution)/shard_map/ppermute | solution.py:15
  (7 other events, 13.5 us)
Sparse Core Ops, SparseCore 0:
  85.7 45.0 reduce-scatter.2
  205.4 38.2 reduce-scatter.4
